TPU v7x, 512 devices: a whole 4x4x16 slice. The times are simulated.
512 devices in a mesh: clip: 4 (over y), st: 32 (over x_hi, z), fsdp: 4 (over x_lo, core).
Axes of the slice: x: 4 (x_hi: 2, x_lo: 2; x = x_hi * 2 + x_lo), y: 4, z: 16, core: 2. Of those that a mesh axis runs over, the one named last changes fastest.
Arguments:
- clip_tokens: bfloat16 [1024, 128, 1024], P(('clip', 'st'), 'fsdp'), parts along dimension 0, may hold values from -6 to 6
- w_spatial: bfloat16 [9, 1024, 512], P(None, ('st', 'fsdp')), may hold values from -0.0625 to 0.0625
- w_temporal: bfloat16 [3, 512, 1024], P(None, None, ('st', 'fsdp')), may hold values from -0.15625 to 0.15625
- frame_time: int32 [64], P('clip'), parts along dimension 0, may hold values from 0 to 15, each once
- dilation: int32 [32], P('clip'), parts along dimension 0, may hold values from 1 to 3
Outputs:
- block_out: bfloat16 [1024, 128, 1024], P(('clip', 'st'), 'fsdp'), parts along dimension 0
There are 4 independent parts, one for each index of `clip`. A program takes and returns all parts, laid end to end along the dimension named above; an argument that names none is the same for every part. Nothing has to cross between parts.
Inputs may be any that keep to these rules, and one draw needn't show every extreme that they name: frame_time is a permutation of 0 to 15.
All inputs are finite; a program needn't handle non-finite values.
Results may differ from a plain program's by a relative error of at most 0.0049.
Values may be sent and summed in bfloat16 or wider, within the bound.
No kernel may reach another device: no remote copies, remote signals or barrier semaphores. Data moves between devices by JAX's collectives and lax.ppermute only.
A program may use at most 64 MiB of HBM per device.

v0:
```python
import jax
import jax.numpy as jnp
from jax import lax
from jax.sharding import PartitionSpec as P

DGROUPS = 8
FRAMES = 16
ROWS = 16


def padded_2(cells, sides, width):
    for axis, dim in sides:
        count = lax.axis_size(axis)
        ends = count - 1
        head = lax.slice_in_dim(cells, 0, width, axis=dim)
        tail = lax.slice_in_dim(cells, cells.shape[dim] - width, cells.shape[dim], axis=dim)
        cells = jnp.concatenate(
            [
                lax.ppermute(tail, axis, [(i, (i + 1) % count) for i in range(ends)]),
                cells,
                lax.ppermute(head, axis, [((i + 1) % count, i) for i in range(ends)]),
            ],
            axis=dim,
        )
    return cells


def partner(value, axis, distance):
    mask = 2**distance
    pairs = [(source, source ^ mask) for source in range(lax.axis_size(axis))]
    return lax.ppermute(value, axis, pairs)


def shards(clip_tokens, w_spatial, w_temporal, frame_time, dilation):
    rows_dev, cols_dev, channels = clip_tokens.shape
    middle = w_spatial.shape[2]
    group_size = lax.axis_size("st")
    values = clip_tokens.astype(jnp.float32)
    average = jnp.mean(values, axis=-1, keepdims=True)
    kernel_extent = jnp.mean(jnp.square(values - average), axis=-1, keepdims=True)
    normed = ((values - average) * lax.rsqrt(kernel_extent + 1e-06)).astype(jnp.bfloat16)
    widened = padded_2(normed, (("fsdp", 1),), 1)
    blank_row = jnp.zeros((1,) + widened.shape[1:], jnp.bfloat16)
    lower_half = lax.axis_index("st") % 2 == 1
    outgoing = jnp.where(lower_half, widened[:1], widened[-1:])
    incoming = partner(outgoing, "st", 0)
    top_rim = jnp.where(lower_half, incoming, blank_row)
    bottom_rim = jnp.where(lower_half, blank_row, incoming)
    padded = jnp.concatenate([top_rim, widened, bottom_rim], axis=0)
    first_row = lax.axis_index("st") * rows_dev
    in_frame = (first_row + jnp.arange(rows_dev, dtype=jnp.int32)) % ROWS
    windows = []
    for shift_amount in (-1, 0, 1):
        inside = ((in_frame + shift_amount >= 0) & (in_frame + shift_amount < ROWS)).astype(
            jnp.bfloat16
        )
        windows.append(
            padded[1 + shift_amount : 1 + shift_amount + rows_dev] * inside[:, None, None]
        )
    tokens = rows_dev * cols_dev
    initial = jnp.zeros((tokens, middle), jnp.float32)
    running = initial
    portion = lax.all_gather(w_spatial, ("st", "fsdp"), axis=1, tiled=True)
    span = portion.shape[1]
    for row_tap in range(3):
        for column_kernel_tap in range(3):
            patches = windows[row_tap][:, column_kernel_tap : column_kernel_tap + cols_dev, :]
            running = running + jnp.dot(
                patches.reshape(tokens, span),
                portion[3 * row_tap + column_kernel_tap],
                preferred_element_type=jnp.float32,
            )
    hidden = jax.nn.gelu(running).astype(jnp.bfloat16)
    pixel_values = ROWS * cols_dev
    block_length_span = min(tokens, pixel_values) // group_size
    depth_len = tokens // (group_size * block_length_span)
    arrived = lax.all_to_all(
        hidden.reshape(depth_len, group_size, block_length_span, middle),
        "st",
        split_axis=1,
        concat_axis=0,
        tiled=True,
    )
    per_pixel = pixel_values // group_size
    group_width = middle // DGROUPS
    frame_sequence = arrived.reshape(FRAMES, per_pixel, DGROUPS, group_width)
    offsets = (jnp.arange(3, dtype=jnp.int32) - 1)[None, :] * dilation[:, None]
    selector_matrix = (
        frame_time[None, None, None, :]
        == frame_time[None, None, :, None] + offsets[:, :, None, None]
    ).astype(jnp.bfloat16)
    stacked_panels = jnp.einsum(
        "gkfe,epgc->kfpgc", selector_matrix, frame_sequence, preferred_element_type=jnp.float32
    )
    stacked_panels = stacked_panels.astype(jnp.bfloat16).reshape(3, FRAMES * per_pixel, middle)
    portion = lax.all_gather(w_temporal, ("st", "fsdp"), axis=2, tiled=True)
    result = jnp.dot(stacked_panels[0], portion[0], preferred_element_type=jnp.float32)
    result = result + jnp.dot(stacked_panels[1], portion[1], preferred_element_type=jnp.float32)
    mixed_out = (
        result + jnp.dot(stacked_panels[2], portion[2], preferred_element_type=jnp.float32)
    ).astype(jnp.bfloat16)
    returned = lax.all_to_all(
        mixed_out.reshape(group_size, depth_len, 1, block_length_span, channels),
        "st",
        split_axis=0,
        concat_axis=2,
        tiled=True,
    )
    update = returned.reshape(rows_dev, cols_dev, channels)
    return (values + update.astype(jnp.float32)).astype(jnp.bfloat16)


def solution(mesh):
    return jax.shard_map(
        shards,
        mesh=mesh,
        in_specs=(
            P(("clip", "st"), "fsdp", None),
            P(None, ("st", "fsdp"), None),
            P(None, None, ("st", "fsdp")),
            P("clip"),
            P("clip"),
        ),
        out_specs=P(("clip", "st"), "fsdp", None),
        check_vma=False,
    )
```

profile of v0, /device:TPU:32, one launch (start us, length us, event | category | flops | bytes accessed | tf_op | source)
XLA Modules:
  0.0 523.0 jit_solution(9462733615842802531)
XLA Ops:
  6.5 0.7 all-gather.3.cloned.1.call-update
  7.3 0.0 all-gather.5.cloned.1.call-start
  7.3 0.7 all-gather.5.cloned.1.call-update
  8.0 1.2 convert_reduce_fusion
  9.2 1.3 fusion.5
  10.5 1.3 fusion.6
  11.8 0.1 fusion.31
  11.9 1.7 collective-permute-start
  13.7 1.3 collective-permute-start.1
  15.0 3.0 collective-permute-done.1
  18.0 0.2 pad_maximum_fusion.6
  18.3 5.7 %collective-permute-start.2 = (bf16[1,34,1024]{2,1,0:T(8,128)(2,1)S(1)}, bf16[1,34,1024]{2,1,0:T(8,128)(2,1)S(1)}, u32[]{:S(2)}, u32[]{:S(2)}) collective-permute-start(bf16[1,34,1024]{2,1,0:T(8,128)(2,1)S(1)} %slice_select_fusion), channel_id=1, source_target_pairs={{0,4},{4,0},{8,12},{12,8},{16,20},{20,16},{24,28},{28,24},{32,36},... | collective-permute-start | bytes 208904 | tf_op jit(solution)/shard_map/ppermute | solution.py:31
  24.0 3.2 collective-permute-done.2
  27.2 0.7 fusion.10
  27.9 1.2 fusion.30
  29.1 0.3 fusion.29
  29.4 1.1 fusion.28
  30.5 212.5 %all-gather.3.cloned.1.call-done = bf16[9,1024,512]{2,1,0:T(8,128)(2,1)} async-done(((bf16[9,8,512]{2,1,0:T(8,128)(2,1)}), bf16[9,1024,512]{2,1,0:T(8,128)(2,1)}) %all-gather.3.cloned.1.call-update) | async-done | bytes 9437200 | tf_op jit(solution)/shard_map/all_gather | solution.py:63
  243.0 2.0 fusion.9
  244.9 2.4 convolution_add_fusion.9
  247.3 1.7 convolution_add_fusion.8
  249.0 1.7 convolution_add_fusion.7
  250.7 0.4 convolution_add_fusion.6
  251.1 0.4 convolution_add_fusion.5
  251.6 0.4 convolution_add_fusion.4
  252.0 0.4 convolution_add_fusion.3
  252.5 0.6 copy-done.3
  253.1 1.3 fusion.20
  254.3 11.1 %all-to-all-start = ((bf16[1,32,8,512]{3,2,0,1:T(8,128)(2,1)}), bf16[1,32,8,512]{3,2,0,1:T(8,128)(2,1)S(1)}, u32[]{:S(2)}, u32[]{:S(2)}) async-start(bf16[1,32,8,512]{3,2,0,1:T(8,128)(2,1)} %fusion.20), calls=%async_computation | async-start | bytes 524288 | tf_op jit(solution)/shard_map/all_to_all | solution.py:77
  265.5 0.1 broadcast_multiply_fusion.1
  265.6 0.1 broadcast_add_fusion
  265.7 21.6 %all-to-all-done = bf16[1,32,8,512]{3,2,0,1:T(8,128)(2,1)S(1)} async-done(((bf16[1,32,8,512]{3,2,0,1:T(8,128)(2,1)}), bf16[1,32,8,512]{3,2,0,1:T(8,128)(2,1)S(1)}, u32[]{:S(2)}, u32[]{:S(2)}) %all-to-all-start) | async-done | bytes 262176 | tf_op jit(solution)/shard_map/all_to_all | solution.py:77
  287.3 0.3 reshape.149
  287.6 0.9 fusion
  288.4 0.3 fusion.27
  288.7 0.3 copy.12
  289.1 0.3 squeeze.54
  289.4 0.3 copy.13
  289.7 0.3 squeeze.56
  290.1 0.3 copy.14
  290.4 0.3 squeeze.58
  290.7 176.7 %all-gather.5.cloned.1.call-done = bf16[3,512,1024]{1,2,0:T(8,128)(2,1)} async-done(((bf16[3,512,8]{1,2,0:T(8,128)(2,1)}), bf16[3,512,1024]{1,2,0:T(8,128)(2,1)}) %all-gather.5.cloned.1.call-update) | async-done | bytes 3145744 | tf_op jit(solution)/shard_map/all_gather | solution.py:96
  467.4 1.7 fusion.8
  469.1 1.7 convolution_add_fusion.1
  470.8 0.0 copy-start
  470.8 1.7 fusion.4
  472.6 42.6 %all_to_all.8 = bf16[32,1,1,8,1024]{4,3,2,1,0:T(8,128)(2,1)S(1)} all-to-all(bf16[32,1,1,8,1024]{4,3,2,1,0:T(8,128)(2,1)S(1)} %fusion.4), channel_id=1, replica_groups=mesh['clip'=4,'st'=32,'fsdp'=4] {'st'}, dimensions={0} | all-to-all | bytes 1048576 | tf_op jit(solution)/shard_map/all_to_all | solution.py:102
  515.2 1.0 fusion.7
  (19 shorter events, 0.1 us)
Async XLA Ops:
  6.5 236.4 %all-gather.3.cloned.1.call-start = ((), (), s32[]{:S(2)}) async-start(), calls=%async_computation.2 | async-start | bytes 9510912 | tf_op jit(solution)/shard_map/all_gather | solution.py:63
  7.3 460.2 %all-gather.5.cloned.1.call-start = ((), (), s32[]{:S(2)}) async-start(), calls=%async_computation.3 | async-start | bytes 3170304 | tf_op jit(solution)/shard_map/all_gather | solution.py:96
  11.9 3.1 collective-permute-start
  13.7 4.4 collective-permute-start.1
  18.3 8.9 %collective-permute-start.2 = (bf16[1,34,1024]{2,1,0:T(8,128)(2,1)S(1)}, bf16[1,34,1024]{2,1,0:T(8,128)(2,1)S(1)}, u32[]{:S(2)}, u32[]{:S(2)}) collective-permute-start(bf16[1,34,1024]{2,1,0:T(8,128)(2,1)S(1)} %slice_select_fusion), channel_id=1, source_target_pairs={{0,4},{4,0},{8,12},{12,8},{16,20},{20,16},{24,28},{28,24},{32,36},... | collective-permute-start | bytes 208904 | tf_op jit(solution)/shard_map/ppermute | solution.py:31
  242.9 2.0 copy-start.2
  242.9 7.7 %copy-start.1 = (bf16[9,1024,512]{2,1,0:T(8,128)(2,1)S(1)}, bf16[9,1024,512]{2,1,0:T(8,128)(2,1)}, u32[]{:S(2)}) copy-start(bf16[9,1024,512]{2,1,0:T(8,128)(2,1)} %all-gather.3.cloned.1.call-done) | copy-start | bytes 28311556
  252.0 1.0 copy-start.3
  253.1 12.4 %copy-start.5 = (s32[8]{0:T(128)S(1)}, s32[8]{0:T(128)}, u32[]{:S(2)}) copy-start(s32[8]{0:T(128)} %param.9) | copy-start | bytes 100
  253.1 12.5 %copy-start.4 = (s32[16]{0:T(128)S(1)}, s32[16]{0:T(128)}, u32[]{:S(2)}) copy-start(s32[16]{0:T(128)} %param.8) | copy-start | bytes 196
  254.3 33.0 %all-to-all-start = ((bf16[1,32,8,512]{3,2,0,1:T(8,128)(2,1)}), bf16[1,32,8,512]{3,2,0,1:T(8,128)(2,1)S(1)}, u32[]{:S(2)}, u32[]{:S(2)}) async-start(bf16[1,32,8,512]{3,2,0,1:T(8,128)(2,1)} %fusion.20), calls=%async_computation | async-start | bytes 524288 | tf_op jit(solution)/shard_map/all_to_all | solution.py:77
  470.8 44.4 %copy-start = (bf16[8,32,1024]{2,1,0:T(8,128)(2,1)S(1)}, bf16[8,32,1024]{2,1,0:T(8,128)(2,1)}, u32[]{:S(2)}) copy-start(bf16[8,32,1024]{2,1,0:T(8,128)(2,1)} %param.5) | copy-start | bytes 1572868
Sparse Core Ops, SparseCore 0:
  9.5 233.3 all-gather.2
  245.1 222.2 all-gather.4
where the time goes:
time: 524 us; the launch traced here: 523 us
  waiting for transfers between devices  418 us (80%)
  blocking collectives  42.6 us (8%)
  starting transfers between devices  19.9 us (4%)
  matrix products  16.7 us (3%)
  between operations  13.7 us (3%)
  other arithmetic  5.9 us (1%)
  local copies, waits for them, and re-layouts  5.82 us (1%)
    all_gather x1, waiting for transfers between devices, shards(): portion = lax.all_gather(w_spatial, ('st', 'fsdp'), axis=1, tiled=True)  212 us
    all_gather x1, waiting for transfers between devices, shards(): portion = lax.all_gather(w_temporal, ('st', 'fsdp'), axis=2, tiled=True)  177 us
    all_to_all x1, blocking collectives, shards(): lax.all_to_all(mixed_out.reshape(group_size, depth_len, 1, block_length_s...  42.6 us
    all_to_all x1, waiting for transfers between devices, shards(): lax.all_to_all(hidden.reshape(depth_len, group_size, block_length_span, m...  21.6 us
    all_to_all x1, starting transfers between devices, shards(): lax.all_to_all(hidden.reshape(depth_len, group_size, block_length_span, m...  11.1 us
    dot_general x9, matrix products, shards(): jnp.dot(patches.reshape(tokens, span), portion[3 * row_tap + column_kerne...  10.7 us
  transfers between devices with their start and end apart: 6, of which 5 were waited for; matrix products, arithmetic and copies ran while one was open for 4% of the time, Pallas kernels for 0%

commit v1 on v0

--- a/solution.py
+++ b/solution.py
@@ -6,6 +6,11 @@
 DGROUPS = 8
 FRAMES = 16
 ROWS = 16
+
+
+def exchange_gather(x, axis, d):
+    outgoing = jnp.stack([x] * lax.axis_size(axis))
+    return jnp.concatenate(lax.all_to_all(outgoing, axis, 0, 0), axis=d)
 
 
 def padded_2(cells, sides, width):
@@ -60,7 +65,7 @@
     tokens = rows_dev * cols_dev
     initial = jnp.zeros((tokens, middle), jnp.float32)
     running = initial
-    portion = lax.all_gather(w_spatial, ("st", "fsdp"), axis=1, tiled=True)
+    portion = exchange_gather(w_spatial, ("st", "fsdp"), 1)
     span = portion.shape[1]
     for row_tap in range(3):
         for column_kernel_tap in range(3):

time: 524 us -> 566 us (1.080)
  the two profiles are of different devices: /device:TPU:32 before, /device:TPU:58 now
where the time goes in v1:
time: 566 us; the launch traced here: 565 us
  waiting for transfers between devices  432 us (76%)
  starting transfers between devices  46.5 us (8%)
  blocking collectives  37.6 us (7%)
  matrix products  22 us (4%)
  between operations  13.8 us (2%)
  local copies, waits for them, and re-layouts  10.4 us (2%)
    ppermute x1, waiting for transfers between devices, partner(): return lax.ppermute(value, axis, pairs)  380 us
    all_to_all x1, blocking collectives, shards(): lax.all_to_all(mixed_out.reshape(group_size, depth_len, 1, block_length_s...  37.6 us
    all_to_all x1, waiting for transfers between devices, exchange_gather(): return jnp.concatenate(lax.all_to_all(outgoing, axis, 0, 0), axis=d)  23.7 us
    all_to_all x1, waiting for transfers between devices, shards(): lax.all_to_all(hidden.reshape(depth_len, group_size, block_length_span, m...  22.5 us
    all_to_all x1, starting transfers between devices, exchange_gather(): return jnp.concatenate(lax.all_to_all(outgoing, axis, 0, 0), axis=d)  19.5 us
    all_to_all x1, starting transfers between devices, shards(): lax.all_to_all(hidden.reshape(depth_len, group_size, block_length_span, m...  19.5 us
    dot_general x9, matrix products, shards(): jnp.dot(patches.reshape(tokens, span), portion[3 * row_tap + column_kerne...  16.1 us
  transfers between devices with their start and end apart: 6, of which 4 were waited for; matrix products, arithmetic and copies ran while one was open for 4% of the time, Pallas kernels for 0%

profile of v1, /device:TPU:58, one launch (start us, length us, event | category | flops | bytes accessed | tf_op | source)
XLA Modules:
  0.0 565.0 jit_solution(4320037018576249620)
XLA Ops:
  6.5 5.1 stack.2
  11.7 19.5 %all-to-all-start = ((bf16[128,9,8,512]{3,2,1,0:T(8,128)(2,1)}), bf16[128,9,8,512]{3,2,1,0:T(8,128)(2,1)}, u32[]{:S(2)}, u32[]{:S(2)}) async-start(bf16[128,9,8,512]{3,2,1,0:T(8,128)(2,1)} %stack.2), calls=%async_computation | async-start | bytes 18874368 | tf_op jit(solution)/shard_map/all_to_all | solution.py:13
  31.2 0.0 all-gather.2.cloned.1.call-start
  31.2 0.7 all-gather.2.cloned.1.call-update
  31.9 0.1 convert_reduce_fusion
  32.1 0.3 fusion.5
  32.4 0.3 fusion.6
  32.7 0.1 fusion.31
  32.7 2.1 collective-permute-start
  34.8 3.5 collective-permute-start.1
  38.3 4.7 collective-permute-done
  43.1 0.2 pad_maximum_fusion.6
  43.3 1.9 collective-permute-start.2
  45.3 380.4 %collective-permute-done.2 = bf16[1,34,1024]{2,1,0:T(8,128)(2,1)S(1)} collective-permute-done((bf16[1,34,1024]{2,1,0:T(8,128)(2,1)S(1)}, bf16[1,34,1024]{2,1,0:T(8,128)(2,1)S(1)}, u32[]{:S(2)}, u32[]{:S(2)}) %collective-permute-start.2) | collective-permute-done | bytes 69664 | tf_op jit(solution)/shard_map/ppermute | solution.py:36
  425.7 0.7 fusion.10
  426.4 1.3 fusion.30
  427.7 0.3 fusion.29
  427.9 1.1 fusion.28
  429.0 23.7 %all-to-all-done = bf16[128,9,8,512]{3,2,1,0:T(8,128)(2,1)} async-done(((bf16[128,9,8,512]{3,2,1,0:T(8,128)(2,1)}), bf16[128,9,8,512]{3,2,1,0:T(8,128)(2,1)}, u32[]{:S(2)}, u32[]{:S(2)}) %all-to-all-start) | async-done | bytes 9437216 | tf_op jit(solution)/shard_map/all_to_all | solution.py:13
  452.7 1.9 fusion.9
  454.6 0.0 copy-start.1
  454.6 1.7 convolution_add_fusion.9
  456.3 1.7 convolution_add_fusion.8
  458.0 1.7 convolution_add_fusion.7
  459.6 1.7 convolution_add_fusion.6
  461.3 1.7 convolution_add_fusion.5
  463.0 1.7 convolution_add_fusion.4
  464.6 1.7 convolution_add_fusion.3
  466.4 2.5 fusion.20
  468.9 19.5 %all-to-all-start.1 = ((bf16[1,32,8,512]{3,2,0,1:T(8,128)(2,1)}), bf16[1,32,8,512]{3,2,0,1:T(8,128)(2,1)S(1)}, u32[]{:S(2)}, u32[]{:S(2)}) async-start(bf16[1,32,8,512]{3,2,0,1:T(8,128)(2,1)} %fusion.20), calls=%async_computation.1 | async-start | bytes 524288 | tf_op jit(solution)/shard_map/all_to_all | solution.py:82
  488.4 0.1 broadcast_multiply_fusion.1
  488.5 0.1 broadcast_add_fusion
  488.5 22.5 %all-to-all-done.1 = bf16[1,32,8,512]{3,2,0,1:T(8,128)(2,1)S(1)} async-done(((bf16[1,32,8,512]{3,2,0,1:T(8,128)(2,1)}), bf16[1,32,8,512]{3,2,0,1:T(8,128)(2,1)S(1)}, u32[]{:S(2)}, u32[]{:S(2)}) %all-to-all-start.1) | async-done | bytes 262176 | tf_op jit(solution)/shard_map/all_to_all | solution.py:82
  511.0 0.3 reshape.174
  511.3 0.9 fusion
  512.1 0.3 fusion.27
  512.4 0.3 copy.12
  512.8 0.3 squeeze.54
  513.1 0.3 copy.13
  513.4 0.3 squeeze.56
  513.8 0.3 copy.14
  514.1 0.3 squeeze.58
  514.4 0.0 all-gather.2.cloned.1.call-done
  514.5 1.7 fusion.8
  516.2 1.7 convolution_add_fusion.1
  517.9 1.7 fusion.4
  519.6 37.6 %all_to_all.23 = bf16[32,1,1,8,1024]{4,3,2,1,0:T(8,128)(2,1)S(1)} all-to-all(bf16[32,1,1,8,1024]{4,3,2,1,0:T(8,128)(2,1)S(1)} %fusion.4), channel_id=1, replica_groups=mesh['clip'=4,'st'=32,'fsdp'=4] {'st'}, dimensions={0} | all-to-all | bytes 1048576 | tf_op jit(solution)/shard_map/all_to_all | solution.py:107
  557.2 1.0 fusion.7
  (19 shorter events, 0.1 us)
Async XLA Ops:
  11.7 20.3 %copy-start = (bf16[8,32,1024]{2,1,0:T(8,128)(2,1)S(1)}, bf16[8,32,1024]{2,1,0:T(8,128)(2,1)}, u32[]{:S(2)}) copy-start(bf16[8,32,1024]{2,1,0:T(8,128)(2,1)} %param.5) | copy-start | bytes 1572868
  11.7 441.0 %all-to-all-start = ((bf16[128,9,8,512]{3,2,1,0:T(8,128)(2,1)}), bf16[128,9,8,512]{3,2,1,0:T(8,128)(2,1)}, u32[]{:S(2)}, u32[]{:S(2)}) async-start(bf16[128,9,8,512]{3,2,1,0:T(8,128)(2,1)} %stack.2), calls=%async_computation | async-start | bytes 18874368 | tf_op jit(solution)/shard_map/all_to_all | solution.py:13
  31.2 483.3 %all-gather.2.cloned.1.call-start = ((), (), s32[]{:S(2)}) async-start(), calls=%async_computation.3 | async-start | bytes 3170304 | tf_op jit(solution)/shard_map/all_gather | solution.py:101
  32.7 10.3 %collective-permute-start = (bf16[8,1,1024]{2,1,0:T(2,128)(2,1)S(1)}, bf16[8,1,1024]{2,1,0:T(2,128)(2,1)S(1)}, u32[]{:S(2)}, u32[]{:S(2)}) collective-permute-start(bf16[8,1,1024]{2,1,0:T(2,128)(2,1)S(1)} %get-tuple-element.20), channel_id=1, source_target_pairs={{0,1},{1,2},{2,3},{4,5},{5,6},{6,7},{8,9},{9,10},{10,11},{12,13},{... | collective-permute-start | bytes 49160 | tf_op jit(solution)/shard_map/ppermute | solution.py:24
  34.8 8.3 %collective-permute-start.1 = (bf16[8,1,1024]{2,1,0:T(2,128)(2,1)S(1)}, bf16[8,1,1024]{2,1,0:T(2,128)(2,1)S(1)}, u32[]{:S(2)}, u32[]{:S(2)}) collective-permute-start(bf16[8,1,1024]{2,1,0:T(2,128)(2,1)S(1)} %get-tuple-element.21), channel_id=1, source_target_pairs={{1,0},{2,1},{3,2},{5,4},{6,5},{7,6},{9,8},{10,9},{11,10},{13,12},{... | collective-permute-start | bytes 49160 | tf_op jit(solution)/shard_map/ppermute | solution.py:26
  43.3 382.3 %collective-permute-start.2 = (bf16[1,34,1024]{2,1,0:T(8,128)(2,1)S(1)}, bf16[1,34,1024]{2,1,0:T(8,128)(2,1)S(1)}, u32[]{:S(2)}, u32[]{:S(2)}) collective-permute-start(bf16[1,34,1024]{2,1,0:T(8,128)(2,1)S(1)} %slice_select_fusion), channel_id=1, source_target_pairs={{0,4},{4,0},{8,12},{12,8},{16,20},{20,16},{24,28},{28,24},{32,36},... | collective-permute-start | bytes 208904 | tf_op jit(solution)/shard_map/ppermute | solution.py:36
  452.7 1.9 copy-start.2
  454.6 1.7 copy-start.1
  464.6 1.7 copy-start.3
  466.4 22.0 %copy-start.5 = (s32[8]{0:T(128)S(1)}, s32[8]{0:T(128)}, u32[]{:S(2)}) copy-start(s32[8]{0:T(128)} %param.9) | copy-start | bytes 100
  466.4 22.1 %copy-start.4 = (s32[16]{0:T(128)S(1)}, s32[16]{0:T(128)}, u32[]{:S(2)}) copy-start(s32[16]{0:T(128)} %param.8) | copy-start | bytes 196
  468.9 42.1 %all-to-all-start.1 = ((bf16[1,32,8,512]{3,2,0,1:T(8,128)(2,1)}), bf16[1,32,8,512]{3,2,0,1:T(8,128)(2,1)S(1)}, u32[]{:S(2)}, u32[]{:S(2)}) async-start(bf16[1,32,8,512]{3,2,0,1:T(8,128)(2,1)} %fusion.20), calls=%async_computation.1 | async-start | bytes 524288 | tf_op jit(solution)/shard_map/all_to_all | solution.py:82
Sparse Core Ops, SparseCore 0:
  34.2 342.1 all-gather.1
